TPU v7x, 32 devices: a whole 2x2x4 slice. The times are simulated.
32 devices in a mesh: grp: 2 (over x), smp: 16 (over z, y, core).
Axes of the slice: x: 2, y: 2, z: 4, core: 2. Of those that a mesh axis runs over, the one named last changes fastest.
Arguments:
- state: bfloat16 [512, 16, 1024], P(('grp', 'smp')), parts along dimension 0, may hold values from -40 to 40
- unit_slot: int32 [512, 64], P(('grp', 'smp')), parts along dimension 0, may hold values from 0 to 511
- token_count: int32 [512], P(('grp', 'smp')), parts along dimension 0, may hold values from 48 to 64, as said below
- session: int32 [512], P(('grp', 'smp')), parts along dimension 0, may hold values from 0 to 15, as said below
- session_row: int32 [32], P('grp'), parts along dimension 0, may hold values from 0 to 15, as said below
- unit_count: int32 [16], replicated, may hold values from 128 to 512, as said below
- panels: bfloat16 [16, 512, 1024], P('smp'), may hold values from -40 to 40
- memory_key: bfloat16 [512, 1024], P(('grp', 'smp')), parts along dimension 0, may hold values from -240 to 240
- memory_value: bfloat16 [512, 1024], P(('grp', 'smp')), parts along dimension 0, may hold values from -24 to 24
- q1_weight: bfloat16 [1024, 1024], replicated, may hold values from -0.1875 to 0.1875
- o1_weight: bfloat16 [1024, 1024], replicated, may hold values from -0.1875 to 0.1875
- kv_weight: bfloat16 [1024, 2048], replicated, may hold values from -6 to 6
- q2_weight: bfloat16 [1024, 1024], replicated, may hold values from -0.1875 to 0.1875
- o2_weight: bfloat16 [1024, 1024], replicated, may hold values from -0.1875 to 0.1875
Outputs:
- latent_out: bfloat16 [512, 16, 1024], P(('grp', 'smp')), parts along dimension 0
There are 2 independent parts, one for each index of `grp`. A program takes and returns all parts, laid end to end along the dimension named above; an argument that names none is the same for every part. Nothing has to cross between parts.
Inputs may be any that keep to these rules, and one draw needn't show every extreme that they name: The panel row of session s is session_row[s]; it lies on the device of index session_row[s]. session_row is a permutation. The 16 samples of one device have sessions on 16 different devices; one device holds the session of one sample on every device. `token_count`: some sample on every device has 64 tokens. `unit_count`: some panel row has 512 units.
All inputs are finite; a program needn't handle non-finite values.
Results may differ from a plain program's by a relative error of at most 0.007.
The roundings to bfloat16 on the way count: a program that leaves them out, or rounds other values in their place, can miss the bound.
Values may be sent and summed in bfloat16 or wider, within the bound.
No kernel may reach another device: no remote copies, remote signals or barrier semaphores. Data moves between devices by JAX's collectives and lax.ppermute only.
A program may use at most 128 MiB of HBM per device.

v0:
```python
import jax
import jax.numpy as jnp
from jax import lax
from jax.sharding import PartitionSpec as P

HEAD_DIM = 64
masked_score = -1e30


def normed(values):
    wide = values.astype(jnp.float32)
    return (wide * lax.rsqrt(jnp.mean(wide * wide, axis=-1, keepdims=True) + 1e-05)).astype(
        jnp.bfloat16
    )


def attend(queries, key_rows, value_rows, live_tokens):
    samples, latents, head_count, head_size = queries.shape
    spike_scores = jnp.einsum(
        "blhd,bkhd->bhlk", queries, key_rows, preferred_element_type=jnp.float32
    ) * HEAD_DIM ** (-0.5)
    spike_scores = jnp.where(live_tokens[:, None, None, :], spike_scores, masked_score)
    spike_max = jnp.max(spike_scores, axis=-1, keepdims=True)
    spike_exp = jnp.exp(spike_scores - spike_max)
    denominator = jnp.transpose(jnp.sum(spike_exp, axis=-1, keepdims=True), (0, 2, 1, 3))
    spike_mix = (
        jnp.einsum(
            "bhlk,bkhd->blhd",
            spike_exp.astype(jnp.bfloat16),
            value_rows,
            preferred_element_type=jnp.float32,
        )
        / denominator
    )
    return spike_mix.reshape(samples, latents, head_count * head_size).astype(jnp.bfloat16)


def per_device(
    state,
    unit_slot,
    token_count,
    session,
    session_row,
    unit_count,
    panels,
    memory_key,
    memory_value,
    q1_weight,
    o1_weight,
    kv_weight,
    q2_weight,
    o2_weight,
):
    local_samples, latents, model_width = state.shape
    token_total = unit_slot.shape[1]
    owners = lax.axis_size("smp")
    sess_dev, unit_total = (panels.shape[0], panels.shape[1])
    head_count = model_width // HEAD_DIM
    session_ids = jnp.arange(session_row.shape[0], dtype=jnp.int32)
    panel_row = jnp.sum(
        jnp.where(session[:, None] == session_ids[None, :], session_row[None, :], 0), axis=1
    )
    unit_limit = jnp.sum(
        jnp.where(panel_row[:, None] == session_ids[None, :], unit_count[None, :], 0), axis=1
    )
    owner_rank = panel_row // sess_dev
    token_index = (panel_row % sess_dev * unit_total)[:, None] + unit_slot % unit_limit[:, None]
    slot_pick = owner_rank[None, :] == jnp.arange(owners, dtype=jnp.int32)[:, None]
    request = jnp.sum(jnp.where(slot_pick[:, :, None], token_index[None, :, :], 0), axis=1)
    live_tokens = jnp.arange(token_total, dtype=jnp.int32)[None, :] < token_count[:, None]
    panel_table = panels.reshape(sess_dev * unit_total, model_width)
    arrived = lax.all_to_all(
        panel_table[lax.all_to_all(request, "smp", split_axis=0, concat_axis=0, tiled=True)],
        "smp",
        split_axis=0,
        concat_axis=0,
        tiled=True,
    )
    row_total = local_samples * latents
    flat_state = state.reshape(row_total, model_width)
    queries = jnp.dot(normed(flat_state), q1_weight, preferred_element_type=jnp.float32).astype(
        jnp.bfloat16
    )
    queries = queries.reshape(row_total, head_count, HEAD_DIM)
    running_max = jnp.full((head_count, row_total), masked_score, jnp.float32)
    key_rows = lax.all_gather(memory_key, "smp", axis=0, tiled=True).reshape(
        -1, head_count, HEAD_DIM
    )
    value_rows = lax.all_gather(memory_value, "smp", axis=0, tiled=True).reshape(
        -1, head_count, HEAD_DIM
    )
    scores = jnp.einsum(
        "rhd,khd->hrk", queries, key_rows, preferred_element_type=jnp.float32
    ) * HEAD_DIM ** (-0.5)
    new_max = jnp.maximum(running_max, jnp.max(scores, axis=-1))
    exponent = jnp.exp(scores - new_max[:, :, None])
    denominator = jnp.sum(exponent, axis=-1)
    weighted = jnp.einsum(
        "hrk,khd->hrd",
        exponent.astype(jnp.bfloat16),
        value_rows,
        preferred_element_type=jnp.float32,
    )
    running_max, denominator, weighted = (new_max, denominator, weighted)
    read_mem = (
        jnp.transpose(weighted / denominator[:, :, None], (1, 0, 2))
        .reshape(row_total, model_width)
        .astype(jnp.bfloat16)
    )
    hidden = (
        flat_state.astype(jnp.float32)
        + jnp.dot(read_mem, o1_weight, preferred_element_type=jnp.float32)
    ).astype(jnp.bfloat16)
    queries2 = jnp.dot(normed(hidden), q2_weight, preferred_element_type=jnp.float32).astype(
        jnp.bfloat16
    )
    queries2 = queries2.reshape(local_samples, latents, model_width)
    embed = arrived[owner_rank]
    key_value = jnp.dot(
        normed(embed.reshape(local_samples * token_total, model_width)),
        kv_weight,
        preferred_element_type=jnp.float32,
    ).astype(jnp.bfloat16)
    key_value = key_value.reshape(local_samples, token_total, 2 * model_width)
    key_rows = key_value[:, :, :model_width].reshape(
        local_samples, token_total, head_count, HEAD_DIM
    )
    value_rows = key_value[:, :, model_width:].reshape(
        local_samples, token_total, head_count, HEAD_DIM
    )
    read_spike = attend(
        queries2.reshape(local_samples, latents, head_count, HEAD_DIM),
        key_rows,
        value_rows,
        live_tokens,
    )
    result = hidden.astype(jnp.float32) + jnp.dot(
        read_spike.reshape(row_total, model_width), o2_weight, preferred_element_type=jnp.float32
    )
    return result.astype(jnp.bfloat16).reshape(local_samples, latents, model_width)


def solution(mesh):
    in_specs = (
        P(("grp", "smp"), None, None),
        P(("grp", "smp"), None),
        P(("grp", "smp")),
        P(("grp", "smp")),
        P("grp"),
        P(),
        P("smp", None, None),
        P(("grp", "smp"), None),
        P(("grp", "smp"), None),
        P(),
        P(),
        P(),
        P(),
        P(),
    )
    out_specs = P(("grp", "smp"), None, None)
    return jax.shard_map(
        per_device, mesh=mesh, in_specs=in_specs, out_specs=out_specs, check_vma=False
    )
```

profile of v0, /device:TPU:0, one launch (start us, length us, event | category | flops | bytes accessed | tf_op | source)
XLA Modules:
  0.0 167.4 jit_solution(13503824719128611106)
XLA Ops:
  0.0 0.0 copy-start
  0.0 1.0 select_reduce_fusion.2
  1.0 0.8 select_reduce_fusion.1
  1.9 0.9 add_select_fusion
  2.8 0.7 select_reduce_fusion
  3.5 7.4 %all-to-all-start = ((s32[16,1,64]{2,1,0:T(1,128)}), s32[16,1,64]{2,1,0:T(1,128)S(1)}, u32[]{:S(2)}, u32[]{:S(2)}) async-start(s32[16,1,64]{2,1,0:T(1,128)} %bitcast.9), calls=%async_computation | async-start | bytes 16384 | tf_op jit(solution)/shard_map/all_to_all | solution.py:73
  10.9 1.2 multiply_reduce_fusion.2
  12.1 5.1 %all-to-all-done = s32[16,1,64]{2,1,0:T(1,128)S(1)} async-done(((s32[16,1,64]{2,1,0:T(1,128)}), s32[16,1,64]{2,1,0:T(1,128)S(1)}, u32[]{:S(2)}, u32[]{:S(2)}) %all-to-all-start) | async-done | bytes 4128 | tf_op jit(solution)/shard_map/all_to_all | solution.py:73
  17.2 0.1 reshape.192
  17.3 7.4 %gather_fusion = bf16[1024,1024]{1,0:T(8,128)(2,1)} fusion(bf16[512,1024]{1,0:T(8,128)(2,1)} %bitcast.57, s32[1024]{0:T(1024)S(1)} %broadcast_clamp_fusion), kind=kCustom, calls=%fused_computation | custom fusion | bytes 4198400 | tf_op jit(solution)/shard_map/gather | solution.py:73
  24.7 0.0 copy-start.1
  24.7 4.6 %all-to-all-start.1 = ((bf16[16,64,1024]{2,1,0:T(8,128)(2,1)}), bf16[16,64,1024]{2,1,0:T(8,128)(2,1)}, u32[]{:S(2)}, u32[]{:S(2)}) async-start(bf16[16,64,1024]{2,1,0:T(8,128)(2,1)} %bitcast.58), calls=%async_computation.1 | async-start | bytes 4194304 | tf_op jit(solution)/shard_map/all_to_all | solution.py:72
  29.3 0.1 rsqrt.31
  29.4 0.0 copy-done.1
  29.4 0.2 fusion.31
  29.5 0.0 copy-start.5
  29.6 3.1 %convolution_convert_fusion.2 = bf16[256,1024]{1,0:T(8,128)(2,1)} fusion(bf16[256,1024]{1,0:T(8,128)(2,1)S(1)} %fusion.31, bf16[1024,1024]{1,0:T(8,128)(2,1)} %param.23), kind=kOutput, calls=%fused_computation.31 | convolution fusion | flops 537133056 | bytes 3145728 | tf_op jit(solution)/shard_map/dot_general | solution.py:81
  32.7 0.0 copy-start.6
  32.7 1.2 copy.36
  33.9 0.0 copy-done.5
  33.9 52.9 %all_gather.6 = bf16[256,1024]{1,0:T(8,128)(2,1)} all-gather(bf16[16,1024]{1,0:T(8,128)(2,1)S(1)} %copy-done.5), channel_id=1, replica_groups=mesh['grp'=2,'smp'=16] {'smp'}, dimensions={0}, use_global_device_ids=true | all-gather | bytes 557056 | tf_op jit(solution)/shard_map/all_gather | solution.py:86
  86.8 2.0 %copy.37 = bf16[256,1024]{0,1:T(8,128)(2,1)} copy(bf16[256,1024]{1,0:T(8,128)(2,1)} %all_gather.6) | data formatting | bytes 1048576 | tf_op jit(solution)/shard_map/all_gather | solution.py:86
  88.9 0.0 copy-done.6
  88.9 25.8 %all_gather.7 = bf16[256,1024]{1,0:T(8,128)(2,1)} all-gather(bf16[16,1024]{1,0:T(8,128)(2,1)S(1)} %copy-done.6), channel_id=1, replica_groups=mesh['grp'=2,'smp'=16] {'smp'}, dimensions={0}, use_global_device_ids=true | all-gather | bytes 557056 | tf_op jit(solution)/shard_map/all_gather | solution.py:89
  114.7 2.0 %copy.38 = bf16[256,1024]{0,1:T(8,128)(2,1)} copy(bf16[256,1024]{1,0:T(8,128)(2,1)} %all_gather.7) | data formatting | bytes 1048576 | tf_op jit(solution)/shard_map/all_gather | solution.py:89
  116.8 1.8 %multiply_reduce_fusion.1 = (f32[16,256]{1,0:T(8,128)S(1)}, f32[16,256,256]{1,2,0:T(8,128)S(1)}) fusion(bf16[256,16,64]{0,2,1:T(8,128)(2,1)S(1)} %bitcast.61, bf16[256,16,64]{0,2,1:T(8,128)(2,1)} %bitcast.62), kind=kOutput, calls=%fused_computation.10 | convolution fusion | flops 136310784 | bytes 5259264 | tf_op jit(solution)/shard_map/rhd,khd->hrk/dot_general | solution.py:92
  118.6 0.0 copy-start.3
  118.6 0.7 fusion.5
  119.3 0.3 copy-done.3
  119.6 0.9 fusion.25
  120.5 0.0 copy-start.9
  120.5 0.0 copy-done
  120.5 0.8 fusion.28
  121.4 0.0 copy-start.4
  121.4 0.8 copy-done.4
  122.2 0.0 copy-done.9
  122.2 0.0 copy-start.7
  122.2 1.6 convolution_convert_fusion.1
  123.8 1.8 %reshape_reshape.3 = bf16[16,16,16,64]{3,2,1,0:T(8,128)(2,1)S(1)} reshape(bf16[256,1024]{1,0:T(8,128)(2,1)} %convolution_convert_fusion.1) | data formatting | bytes 1048576 | tf_op jit(solution)/shard_map/reshape;reshape | solution.py:132
  125.5 0.0 copy-done.7
  125.6 0.1 iota_compare_fusion
  125.6 0.0 all-to-all-done.1
  125.6 3.6 %gather_fusion.1 = bf16[16,64,1024]{2,1,0:T(8,128)(2,1)} fusion(bf16[16,64,1024]{2,1,0:T(8,128)(2,1)} %all-to-all-done.1, s32[1024]{0:T(1024)S(1)} %pad_clamp_fusion), kind=kCustom, calls=%fused_computation.1 | custom fusion | bytes 4194368 | tf_op jit(solution)/shard_map/gather | solution.py:118
  129.2 2.1 %multiply_reduce_fusion = f32[16,64]{1,0:T(8,128)S(1)} fusion(bf16[16,64,1024]{2,1,0:T(8,128)(2,1)} %gather_fusion.1), kind=kLoop, calls=%fused_computation.8 | loop fusion | flops 3144704 | bytes 2101248 | tf_op jit(solution)/shard_map/reduce_sum | solution.py:12
  131.3 0.1 rsqrt.33
  131.4 0.0 copy-start.8
  131.4 2.1 %fusion = bf16[1024,1024]{1,0:T(8,128)(2,1)S(1)} fusion(f32[1024]{0:T(1024)S(1)} %rsqrt.33, bf16[16,64,1024]{2,1,0:T(8,128)(2,1)} %gather_fusion.1), kind=kLoop, calls=%fused_computation.3 | loop fusion | flops 3145728 | bytes 4198400 | tf_op jit(solution)/shard_map/convert_element_type | solution.py:12
  133.5 0.7 copy-done.8
  134.2 4.7 %convolution_convert_fusion = bf16[1024,2048]{1,0:T(8,128)(2,1)S(1)} fusion(bf16[1024,1024]{1,0:T(8,128)(2,1)S(1)} %fusion, bf16[1024,2048]{1,0:T(8,128)(2,1)S(1)} %copy-done.8), kind=kOutput, calls=%fused_computation.11 | convolution fusion | flops 4297064448 | bytes 10485760 | tf_op jit(solution)/shard_map/dot_general | solution.py:119
  138.9 2.6 %fusion.43 = (bf16[16,64,1024]{2,1,0:T(8,128)(2,1)}, bf16[16,64,1024]{2,1,0:T(8,128)(2,1)}) fusion(bf16[16,64,2048]{2,1,0:T(8,128)(2,1)S(1)} %bitcast.60), kind=kLoop, calls=%fused_computation.68 | loop fusion | bytes 8388608 | tf_op jit(solution)/shard_map/slice | solution.py:125
  141.5 6.4 %reshape.186 = bf16[16,64,16,64]{3,2,1,0:T(8,128)(2,1)} reshape(bf16[16,64,1024]{2,1,0:T(8,128)(2,1)} %get-tuple-element.5) | data formatting | bytes 4194304 | tf_op jit(solution)/shard_map/reshape | solution.py:125
  147.9 6.4 %reshape.185 = bf16[16,64,16,64]{3,2,1,0:T(8,128)(2,1)} reshape(bf16[16,64,1024]{2,1,0:T(8,128)(2,1)} %get-tuple-element.6) | data formatting | bytes 4194304 | tf_op jit(solution)/shard_map/reshape | solution.py:128
  154.3 0.0 copy-start.2
  154.3 4.7 %fusion.12 = (f32[16,16,16]{2,1,0:T(8,128)S(1)}, f32[16,16,16,64]{3,2,1,0:T(8,128)S(1)}) fusion(pred[16,64]{1,0:T(8,128)(4,1)S(1)} %iota_compare_fusion, bf16[16,64,16,64]{3,2,1,0:T(8,128)(2,1)} %reshape.186, bf16[16,16,16,64]{3,2,1,0:T(8,128)(2,1)S(1)} %reshape_reshape.3), kind=kOutput, calls=%fused_computation.21 | convolution fusion | flops 34336768 | bytes 3687424 | tf_op jit(solution)/shard_map/blhd,bkhd->bhlk/dot_general | solution.py:19
  159.0 1.3 fusion.15
  160.3 0.0 copy-done.2
  160.3 2.0 %fusion.9 = bf16[16,16,16,64]{3,1,2,0:T(8,128)(2,1)S(1)} fusion(bf16[16,64,16,64]{3,2,1,0:T(8,128)(2,1)S(1)} %copy-done.2, f32[16,16,16,64]{3,2,1,0:T(8,128)S(1)} %get-tuple-element.12, f32[16,16,16]{1,2,0:T(8,128)S(1)} %bitcast.65, f32[16,16,16]{2,1,0:T(8,128)S(1)} %get-tuple-element.11, pred[16,64]{1,0:T(8,128)(4,1)S(1)} %iota_compare_fusion), kind=kOutput, calls=%fused_computation.16 | convolution fusion | flops 35127296 | bytes 3703808 | tf_op jit(solution)/shard_map/bhlk,bkhd->blhd/dot_general | solution.py:27
  162.3 0.3 copy.44
  162.6 1.5 convert_element_type.85
  164.1 3.3 %fusion.20 = bf16[256,1024]{1,0:T(8,128)(2,1)} fusion(bf16[256,1024]{1,0:T(8,128)(2,1)} %convert_element_type.85, bf16[1024,1024]{1,0:T(8,128)(2,1)} %param.27, bf16[256,1024]{1,0:T(8,128)(2,1)} %copy-done.4), kind=kOutput, calls=%fused_computation.29 | convolution fusion | flops 537657344 | bytes 3670016 | tf_op jit(solution)/shard_map/dot_general | solution.py:137
  (11 shorter events, 0.1 us)
Async XLA Ops:
  0.0 120.5 %copy-start = (bf16[1024,1024]{1,0:T(8,128)(2,1)S(1)}, bf16[1024,1024]{1,0:T(8,128)(2,1)}, u32[]{:S(2)}) copy-start(bf16[1024,1024]{1,0:T(8,128)(2,1)} %param.24) | copy-start | bytes 6291460
  3.5 13.7 %all-to-all-start = ((s32[16,1,64]{2,1,0:T(1,128)}), s32[16,1,64]{2,1,0:T(1,128)S(1)}, u32[]{:S(2)}, u32[]{:S(2)}) async-start(s32[16,1,64]{2,1,0:T(1,128)} %bitcast.9), calls=%async_computation | async-start | bytes 16384 | tf_op jit(solution)/shard_map/all_to_all | solution.py:73
  24.7 4.7 %copy-start.1 = (bf16[16,16,1024]{2,1,0:T(8,128)(2,1)S(1)}, bf16[16,16,1024]{2,1,0:T(8,128)(2,1)}, u32[]{:S(2)}) copy-start(bf16[16,16,1024]{2,1,0:T(8,128)(2,1)} %param.14) | copy-start | bytes 1572868
  24.7 100.9 %all-to-all-start.1 = ((bf16[16,64,1024]{2,1,0:T(8,128)(2,1)}), bf16[16,64,1024]{2,1,0:T(8,128)(2,1)}, u32[]{:S(2)}, u32[]{:S(2)}) async-start(bf16[16,64,1024]{2,1,0:T(8,128)(2,1)} %bitcast.58), calls=%async_computation.1 | async-start | bytes 4194304 | tf_op jit(solution)/shard_map/all_to_all | solution.py:72
  29.5 4.4 %copy-start.5 = (bf16[16,1024]{1,0:T(8,128)(2,1)S(1)}, bf16[16,1024]{1,0:T(8,128)(2,1)}, u32[]{:S(2)}) copy-start(bf16[16,1024]{1,0:T(8,128)(2,1)} %param.21) | copy-start | bytes 98308
  32.7 56.2 %copy-start.6 = (bf16[16,1024]{1,0:T(8,128)(2,1)S(1)}, bf16[16,1024]{1,0:T(8,128)(2,1)}, u32[]{:S(2)}) copy-start(bf16[16,1024]{1,0:T(8,128)(2,1)} %param.22) | copy-start | bytes 98308
  118.6 1.0 copy-start.3
  120.5 1.7 %copy-start.9 = (bf16[1024,1024]{1,0:T(8,128)(2,1)S(1)}, bf16[1024,1024]{1,0:T(8,128)(2,1)}, u32[]{:S(2)}) copy-start(bf16[1024,1024]{1,0:T(8,128)(2,1)} %param.26) | copy-start | bytes 6291460
  121.4 0.8 copy-start.4
  122.2 3.4 %copy-start.7 = (s32[16]{0:T(128)S(1)}, s32[16]{0:T(128)}, u32[]{:S(2)}) copy-start(s32[16]{0:T(128)} %param.16) | copy-start | bytes 196
  131.4 2.8 %copy-start.8 = (bf16[1024,2048]{1,0:T(8,128)(2,1)S(1)}, bf16[1024,2048]{1,0:T(8,128)(2,1)}, u32[]{:S(2)}) copy-start(bf16[1024,2048]{1,0:T(8,128)(2,1)} %param.25) | copy-start | bytes 12582916
  154.3 6.1 %copy-start.2 = (bf16[16,64,16,64]{3,2,1,0:T(8,128)(2,1)S(1)}, bf16[16,64,16,64]{3,2,1,0:T(8,128)(2,1)}, u32[]{:S(2)}) copy-start(bf16[16,64,16,64]{3,2,1,0:T(8,128)(2,1)} %reshape.185) | copy-start | bytes 6291460
where the time goes:
time: 168 us; the launch traced here: 167 us
  blocking collectives  78.8 us (47%)
  local copies, waits for them, and re-layouts  37.3 us (22%)
  matrix products  22.9 us (14%)
  starting transfers between devices  11.9 us (7%)
  other arithmetic  11.2 us (7%)
  waiting for transfers between devices  5.11 us (3%)
    all_gather x1, blocking collectives, per_device(): lax.all_gather(memory_key, 'smp', axis=0, tiled=True)  52.9 us
    all_gather x1, blocking collectives, per_device(): lax.all_gather(memory_value, 'smp', axis=0, tiled=True)  25.8 us
    gather x1, local copies, waits for them, and re-layouts, per_device(): panel_table[lax.all_to_all(request, 'smp', split_axis=0, concat_axis=0, t...  7.42 us
    all_to_all x1, starting transfers between devices, per_device(): lax.all_to_all(request, 'smp', split_axis=0, concat_axis=0, tiled=True)  7.39 us
    reshape x1, local copies, waits for them, and re-layouts, per_device(): key_value[:, :, :model_width]  6.37 us
    reshape x1, local copies, waits for them, and re-layouts, per_device(): key_value[:, :, model_width:]  6.37 us
    all_to_all x1, waiting for transfers between devices, per_device(): lax.all_to_all(request, 'smp', split_axis=0, concat_axis=0, tiled=True)  5.11 us
    dot_general x1, matrix products, per_device(): jnp.dot(normed(embed.reshape(local_samples * token_total, model_width)),...  4.71 us
  transfers between devices with their start and end apart: 2, of which 1 were waited for; matrix products, arithmetic and copies ran while one was open for 10% of the time, Pallas kernels for 0%

commit v1 on v0

--- a/solution.py
+++ b/solution.py
@@ -51,6 +51,23 @@
     q2_weight,
     o2_weight,
 ):
+
+    def marks_shape(raw, chip_axis):
+        tmp = lax.axis_size(chip_axis)
+        val = lax.axis_index(chip_axis)
+        z, x_next = (tmp, val)
+        back, f_now = (raw, 1)
+        while f_now < z:
+            block_list = []
+            for q in range(z):
+                block_list.append((q, q ^ f_now))
+            local_part = lax.ppermute(back, chip_axis, block_list)
+            field_out = jnp.concatenate([back, local_part], axis=0)
+            moved = jnp.concatenate([local_part, back], axis=0)
+            back = jnp.where(x_next & f_now == 0, field_out, moved)
+            f_now = 2 * f_now
+        return back
+
     local_samples, latents, model_width = state.shape
     token_total = unit_slot.shape[1]
     owners = lax.axis_size("smp")
@@ -86,9 +103,7 @@
     key_rows = lax.all_gather(memory_key, "smp", axis=0, tiled=True).reshape(
         -1, head_count, HEAD_DIM
     )
-    value_rows = lax.all_gather(memory_value, "smp", axis=0, tiled=True).reshape(
-        -1, head_count, HEAD_DIM
-    )
+    value_rows = marks_shape(memory_value, "smp").reshape(-1, head_count, HEAD_DIM)
     scores = jnp.einsum(
         "rhd,khd->hrk", queries, key_rows, preferred_element_type=jnp.float32
     ) * HEAD_DIM ** (-0.5)

time: 168 us -> 177 us (1.054)
  blocking collectives: 78.8 us -> 57.4 us
  waiting for transfers between devices: 5.11 us -> 22.3 us
  starting transfers between devices: 11.9 us -> 23.6 us
  other arithmetic: 11.2 us -> 13.8 us
  local copies, waits for them, and re-layouts: 37.3 us -> 34.8 us
    all_gather x1 -> x0, blocking collectives: 25.8 us -> none  [per_device(): lax.all_gather(memory_value, 'smp', axis=0, tiled=True)]
    ppermute x0 -> x4, waiting for transfers between devices: none -> 22.3 us  [marks_shape(): local_part = lax.ppermute(back, chip_axis, block_list)]
    ppermute x0 -> x4, starting transfers between devices: none -> 10.5 us  [marks_shape(): local_part = lax.ppermute(back, chip_axis, block_list)]
    all_to_all x1, waiting for transfers between devices: 5.11 us -> 0.01 us  [per_device(): lax.all_to_all(request, 'smp', split_axis=0, concat_axis=0, tiled=True)]
    all_gather x1, blocking collectives: 52.9 us -> 57.4 us  [per_device(): lax.all_gather(memory_key, 'smp', axis=0, tiled=True)]
    dot_general x1, matrix products: 0.87 us -> 3.11 us  [per_device(): jnp.einsum('hrk,khd->hrd', exponent.astype(jnp.bfloat16), value_rows, pre...]
    gather x1, local copies, waits for them, and re-layouts: 7.42 us -> 5.37 us  [per_device(): panel_table[lax.all_to_all(request, 'smp', split_axis=0, concat_axis=0, t...]
    all_gather x1 -> x0, local copies, waits for them, and re-layouts: 2.04 us -> none  [per_device(): lax.all_gather(memory_value, 'smp', axis=0, tiled=True)]
  transfers between devices with their start and end apart: 2 -> 6, of which waited for: 1 -> 3; matrix products, arithmetic and copies ran while one was open for 10% -> 16% of each run, Pallas kernels for 0% -> 0%
where the time goes in v1:
time: 177 us; the launch traced here: 176 us
  blocking collectives  57.4 us (32%)
  local copies, waits for them, and re-layouts  34.8 us (20%)
  matrix products  24.2 us (14%)
  starting transfers between devices  23.6 us (13%)
  waiting for transfers between devices  22.3 us (13%)
  other arithmetic  13.8 us (8%)
    all_gather x1, blocking collectives, per_device(): lax.all_gather(memory_key, 'smp', axis=0, tiled=True)  57.4 us
    ppermute x4, waiting for transfers between devices, marks_shape(): local_part = lax.ppermute(back, chip_axis, block_list)  22.3 us
    ppermute x4, starting transfers between devices, marks_shape(): local_part = lax.ppermute(back, chip_axis, block_list)  10.5 us
    all_to_all x1, starting transfers between devices, per_device(): lax.all_to_all(request, 'smp', split_axis=0, concat_axis=0, tiled=True)  6.91 us
    reshape x1, local copies, waits for them, and re-layouts, per_device(): key_value[:, :, :model_width]  6.37 us
    reshape x1, local copies, waits for them, and re-layouts, per_device(): key_value[:, :, model_width:]  6.37 us
    all_to_all x1, starting transfers between devices, per_device(): lax.all_to_all(panel_table[lax.all_to_all(request, 'smp', split_axis=0, c...  6.19 us
    gather x1, local copies, waits for them, and re-layouts, per_device(): panel_table[lax.all_to_all(request, 'smp', split_axis=0, concat_axis=0, t...  5.37 us
  transfers between devices with their start and end apart: 6, of which 3 were waited for; matrix products, arithmetic and copies ran while one was open for 16% of the time, Pallas kernels for 0%

profile of v1, /device:TPU:0, one launch (start us, length us, event | category | flops | bytes accessed | tf_op | source)
XLA Modules:
  0.0 176.3 jit_solution(9231060530090173269)
XLA Ops:
  0.0 0.0 copy-start
  0.0 0.5 collective-permute-start
  0.5 1.0 select_reduce_fusion.2
  1.5 0.8 select_reduce_fusion.1
  2.4 0.9 add_select_fusion
  3.3 0.7 select_reduce_fusion
  4.0 6.9 %all-to-all-start = ((s32[16,1,64]{2,1,0:T(1,128)}), s32[16,1,64]{2,1,0:T(1,128)S(1)}, u32[]{:S(2)}, u32[]{:S(2)}) async-start(s32[16,1,64]{2,1,0:T(1,128)} %bitcast.13), calls=%async_computation | async-start | bytes 16384 | tf_op jit(solution)/shard_map/all_to_all | solution.py:90
  10.9 1.2 multiply_reduce_fusion.2
  12.1 0.1 rsqrt.31
  12.2 1.2 fusion.31
  13.4 0.0 copy-start.1
  13.4 3.2 %convolution_convert_fusion.2 = bf16[256,1024]{1,0:T(8,128)(2,1)} fusion(bf16[256,1024]{1,0:T(8,128)(2,1)S(1)} %fusion.31, bf16[1024,1024]{1,0:T(8,128)(2,1)} %param.23), kind=kOutput, calls=%fused_computation.31 | convolution fusion | flops 537133056 | bytes 3145728 | tf_op jit(solution)/shard_map/dot_general | solution.py:98
  16.6 2.0 %copy.51 = bf16[256,1024]{0,1:T(8,128)(2,1)} copy(bf16[256,1024]{1,0:T(8,128)(2,1)} %convolution_convert_fusion.2) | data formatting | bytes 1048576 | tf_op jit(solution)/shard_map/convert_element_type | solution.py:98
  18.6 0.0 all-to-all-done
  18.6 0.1 reshape.205
  18.7 5.4 %gather_fusion = bf16[1024,1024]{1,0:T(8,128)(2,1)} fusion(bf16[512,1024]{1,0:T(8,128)(2,1)S(1)} %bitcast.60, s32[1024]{0:T(1024)S(1)} %broadcast_clamp_fusion), kind=kCustom, calls=%fused_computation | custom fusion | bytes 4198400 | tf_op jit(solution)/shard_map/gather | solution.py:90
  24.1 6.2 %all-to-all-start.1 = ((bf16[16,64,1024]{2,1,0:T(8,128)(2,1)}), bf16[16,64,1024]{2,1,0:T(8,128)(2,1)}, u32[]{:S(2)}, u32[]{:S(2)}) async-start(bf16[16,64,1024]{2,1,0:T(8,128)(2,1)} %bitcast.61), calls=%async_computation.1 | async-start | bytes 4194304 | tf_op jit(solution)/shard_map/all_to_all | solution.py:89
  30.3 0.0 copy-done.8
  30.3 57.4 %all_gather.3 = bf16[256,1024]{1,0:T(8,128)(2,1)} all-gather(bf16[16,1024]{1,0:T(8,128)(2,1)S(1)} %copy-done.8), channel_id=1, replica_groups=mesh['grp'=2,'smp'=16] {'smp'}, dimensions={0}, use_global_device_ids=true | all-gather | bytes 557056 | tf_op jit(solution)/shard_map/all_gather | solution.py:103
  87.7 1.2 copy.52
  88.9 0.8 multiply_reduce_fusion.1
  89.7 0.0 copy-start.7
  89.7 0.0 copy-start.9
  89.8 0.7 fusion.5
  90.5 1.2 copy-done.2
  91.6 0.0 collective-permute-done
  91.7 0.2 copy.55
  91.8 0.2 copy.56
  92.0 3.1 %collective-permute-start.1 = (bf16[32,1024]{0,1:T(8,128)(2,1)S(1)}, bf16[32,1024]{0,1:T(8,128)(2,1)S(1)}, u32[]{:S(2)}, u32[]{:S(2)}) collective-permute-start(bf16[32,1024]{0,1:T(8,128)(2,1)S(1)} %broadcast_select_fusion), channel_id=1, source_target_pairs={{0,2},{1,3},{2,0},{3,1},{4,6},{5,7},{6,4},{7,5},{8,10},{9,11},{10,... | collective-permute-start | bytes 196616 | tf_op jit(solution)/shard_map/ppermute | solution.py:64
  95.1 0.1 iota_compare_fusion
  95.2 6.6 %collective-permute-done.1 = bf16[32,1024]{0,1:T(8,128)(2,1)S(1)} collective-permute-done((bf16[32,1024]{0,1:T(8,128)(2,1)S(1)}, bf16[32,1024]{0,1:T(8,128)(2,1)S(1)}, u32[]{:S(2)}, u32[]{:S(2)}) %collective-permute-start.1) | collective-permute-done | bytes 65568 | tf_op jit(solution)/shard_map/ppermute | solution.py:64
  101.8 0.3 maximum_select_fusion.4
  102.1 4.2 %collective-permute-start.2 = (bf16[64,1024]{0,1:T(8,128)(2,1)S(1)}, bf16[64,1024]{0,1:T(8,128)(2,1)S(1)}, u32[]{:S(2)}, u32[]{:S(2)}) collective-permute-start(bf16[64,1024]{0,1:T(8,128)(2,1)S(1)} %maximum_select_fusion.4), channel_id=1, source_target_pairs={{0,4},{1,5},{2,6},{3,7},{4,0},{5,1},{6,2},{7,3},{8,12},{9,13},{10,... | collective-permute-start | bytes 393224 | tf_op jit(solution)/shard_map/ppermute | solution.py:64
  106.3 0.2 copy.53
  106.5 0.2 copy.54
  106.7 5.6 %collective-permute-done.2 = bf16[64,1024]{0,1:T(8,128)(2,1)S(1)} collective-permute-done((bf16[64,1024]{0,1:T(8,128)(2,1)S(1)}, bf16[64,1024]{0,1:T(8,128)(2,1)S(1)}, u32[]{:S(2)}, u32[]{:S(2)}) %collective-permute-start.2) | collective-permute-done | bytes 131104 | tf_op jit(solution)/shard_map/ppermute | solution.py:64
  112.3 0.3 maximum_select_fusion.6
  112.6 2.7 %collective-permute-start.3 = (bf16[128,1024]{0,1:T(8,128)(2,1)S(1)}, bf16[128,1024]{0,1:T(8,128)(2,1)S(1)}, u32[]{:S(2)}, u32[]{:S(2)}) collective-permute-start(bf16[128,1024]{0,1:T(8,128)(2,1)S(1)} %maximum_select_fusion.6), channel_id=1, source_target_pairs={{0,8},{1,9},{2,10},{3,11},{4,12},{5,13},{6,14},{7,15},{8,0},{9,1},... | collective-permute-start | bytes 786440 | tf_op jit(solution)/shard_map/ppermute | solution.py:64
  115.3 0.3 maximum_select_fusion.2
  115.6 0.3 maximum_select_fusion.3
  115.9 0.3 maximum_select_fusion.5
  116.2 10.1 %collective-permute-done.3 = bf16[128,1024]{0,1:T(8,128)(2,1)S(1)} collective-permute-done((bf16[128,1024]{0,1:T(8,128)(2,1)S(1)}, bf16[128,1024]{0,1:T(8,128)(2,1)S(1)}, u32[]{:S(2)}, u32[]{:S(2)}) %collective-permute-start.3) | collective-permute-done | bytes 262176 | tf_op jit(solution)/shard_map/ppermute | solution.py:64
  126.3 3.1 %fusion.25 = bf16[256,16,64]{0,2,1:T(8,128)(2,1)S(1)} fusion(f32[16,256,256]{1,2,0:T(8,128)} %copy-done.2, f32[16,256]{1,0:T(8,128)S(1)} %broadcast_maximum_fusion, bf16[128,16,64]{0,2,1:T(8,128)(2,1)S(1)} %bitcast.74, bf16[128,16,64]{0,2,1:T(8,128)(2,1)S(1)} %maximum_select_fusion.5, f32[256,16]{0,1:T(8,128)S(1)} %bitcast.73, pred[]{:T(512)S(6)} %eq.69), kind=kOutput, calls=%fused_computation.34 | convolution fusion | flops 140247040 | bytes 5275649 | tf_op jit(solution)/shard_map/hrk,khd->hrd/dot_general | solution.py:113
  129.5 0.0 copy-start.11
  129.5 0.8 fusion.28
  130.4 0.8 copy-done.6
  131.2 1.6 convolution_convert_fusion.1
  132.7 1.8 reshape_reshape.3
  134.5 0.0 all-to-all-done.1
  134.5 3.6 %gather_fusion.1 = bf16[16,64,1024]{2,1,0:T(8,128)(2,1)} fusion(bf16[16,64,1024]{2,1,0:T(8,128)(2,1)} %all-to-all-done.1, s32[1024]{0:T(1024)S(1)} %pad_clamp_fusion), kind=kCustom, calls=%fused_computation.1 | custom fusion | bytes 4194368 | tf_op jit(solution)/shard_map/gather | solution.py:133
  138.1 2.1 %multiply_reduce_fusion = f32[16,64]{1,0:T(8,128)S(1)} fusion(bf16[16,64,1024]{2,1,0:T(8,128)(2,1)} %gather_fusion.1), kind=kLoop, calls=%fused_computation.8 | loop fusion | flops 3144704 | bytes 2101248 | tf_op jit(solution)/shard_map/reduce_sum | solution.py:12
  140.2 0.1 rsqrt.33
  140.3 2.1 %fusion = bf16[1024,1024]{1,0:T(8,128)(2,1)S(1)} fusion(f32[1024]{0:T(1024)S(1)} %rsqrt.33, bf16[16,64,1024]{2,1,0:T(8,128)(2,1)} %gather_fusion.1), kind=kLoop, calls=%fused_computation.3 | loop fusion | flops 3145728 | bytes 4198400 | tf_op jit(solution)/shard_map/convert_element_type | solution.py:12
  142.4 0.7 copy-done.10
  143.1 4.7 %convolution_convert_fusion = bf16[1024,2048]{1,0:T(8,128)(2,1)S(1)} fusion(bf16[1024,1024]{1,0:T(8,128)(2,1)S(1)} %fusion, bf16[1024,2048]{1,0:T(8,128)(2,1)S(1)} %copy-done.10), kind=kOutput, calls=%fused_computation.11 | convolution fusion | flops 4297064448 | bytes 10485760 | tf_op jit(solution)/shard_map/dot_general | solution.py:134
  147.8 2.6 %fusion.50 = (bf16[16,64,1024]{2,1,0:T(8,128)(2,1)}, bf16[16,64,1024]{2,1,0:T(8,128)(2,1)}) fusion(bf16[16,64,2048]{2,1,0:T(8,128)(2,1)S(1)} %bitcast.63), kind=kLoop, calls=%fused_computation.84 | loop fusion | bytes 8388608 | tf_op jit(solution)/shard_map/slice | solution.py:140
  150.4 6.4 %reshape.199 = bf16[16,64,16,64]{3,2,1,0:T(8,128)(2,1)} reshape(bf16[16,64,1024]{2,1,0:T(8,128)(2,1)} %get-tuple-element.5) | data formatting | bytes 4194304 | tf_op jit(solution)/shard_map/reshape | solution.py:140
  156.8 6.4 %reshape.198 = bf16[16,64,16,64]{3,2,1,0:T(8,128)(2,1)} reshape(bf16[16,64,1024]{2,1,0:T(8,128)(2,1)} %get-tuple-element.6) | data formatting | bytes 4194304 | tf_op jit(solution)/shard_map/reshape | solution.py:143
  163.2 4.7 %fusion.12 = (f32[16,16,16]{2,1,0:T(8,128)S(1)}, f32[16,16,16,64]{3,2,1,0:T(8,128)S(1)}) fusion(pred[16,64]{1,0:T(8,128)(4,1)S(1)} %iota_compare_fusion, bf16[16,64,16,64]{3,2,1,0:T(8,128)(2,1)} %reshape.199, bf16[16,16,16,64]{3,2,1,0:T(8,128)(2,1)S(1)} %reshape_reshape.3), kind=kOutput, calls=%fused_computation.21 | convolution fusion | flops 34336768 | bytes 3687424 | tf_op jit(solution)/shard_map/blhd,bkhd->bhlk/dot_general | solution.py:19
  167.9 1.3 fusion.15
  169.2 2.0 %fusion.9 = bf16[16,16,16,64]{3,1,2,0:T(8,128)(2,1)S(1)} fusion(bf16[16,64,16,64]{3,2,1,0:T(8,128)(2,1)S(1)} %copy-done.4, f32[16,16,16,64]{3,2,1,0:T(8,128)S(1)} %get-tuple-element.14, f32[16,16,16]{1,2,0:T(8,128)S(1)} %bitcast.71, f32[16,16,16]{2,1,0:T(8,128)S(1)} %get-tuple-element.13, pred[16,64]{1,0:T(8,128)(4,1)S(1)} %iota_compare_fusion), kind=kOutput, calls=%fused_computation.16 | convolution fusion | flops 35127296 | bytes 3703808 | tf_op jit(solution)/shard_map/bhlk,bkhd->blhd/dot_general | solution.py:27
  171.2 0.3 copy.62
  171.5 1.5 convert_element_type.85
  173.0 3.3 %fusion.20 = bf16[256,1024]{1,0:T(8,128)(2,1)} fusion(bf16[256,1024]{1,0:T(8,128)(2,1)} %convert_element_type.85, bf16[1024,1024]{1,0:T(8,128)(2,1)} %param.27, bf16[256,1024]{1,0:T(8,128)(2,1)} %copy-done.6), kind=kOutput, calls=%fused_computation.29 | convolution fusion | flops 537657344 | bytes 3670016 | tf_op jit(solution)/shard_map/dot_general | solution.py:152
  (28 shorter events, 0.1 us)
Async XLA Ops:
  0.0 129.5 %copy-start = (bf16[1024,1024]{1,0:T(8,128)(2,1)S(1)}, bf16[1024,1024]{1,0:T(8,128)(2,1)}, u32[]{:S(2)}) copy-start(bf16[1024,1024]{1,0:T(8,128)(2,1)} %param.24) | copy-start | bytes 6291460
  0.0 91.6 %collective-permute-start = (bf16[16,1024]{1,0:T(8,128)(2,1)}, bf16[16,1024]{1,0:T(8,128)(2,1)S(1)}, u32[]{:S(2)}, u32[]{:S(2)}) collective-permute-start(bf16[16,1024]{1,0:T(8,128)(2,1)} %param.22), channel_id=1, source_target_pairs={{0,1},{1,0},{2,3},{3,2},{4,5},{5,4},{6,7},{7,6},{8,9},{9,8},{10,11... | collective-permute-start | bytes 98312 | tf_op jit(solution)/shard_map/ppermute | solution.py:64
  4.0 14.7 %all-to-all-start = ((s32[16,1,64]{2,1,0:T(1,128)}), s32[16,1,64]{2,1,0:T(1,128)S(1)}, u32[]{:S(2)}, u32[]{:S(2)}) async-start(s32[16,1,64]{2,1,0:T(1,128)} %bitcast.13), calls=%async_computation | async-start | bytes 16384 | tf_op jit(solution)/shard_map/all_to_all | solution.py:90
  13.4 5.3 %copy-start.1 = (bf16[1,512,1024]{2,1,0:T(8,128)(2,1)S(1)}, bf16[1,512,1024]{2,1,0:T(8,128)(2,1)}, u32[]{:S(2)}) copy-start(bf16[1,512,1024]{2,1,0:T(8,128)(2,1)} %param.20) | copy-start | bytes 3145732
  24.1 6.2 %copy-start.8 = (bf16[16,1024]{1,0:T(8,128)(2,1)S(1)}, bf16[16,1024]{1,0:T(8,128)(2,1)}, u32[]{:S(2)}) copy-start(bf16[16,1024]{1,0:T(8,128)(2,1)} %param.21) | copy-start | bytes 98308
  24.1 64.8 %copy-start.5 = (bf16[256,1024]{0,1:T(8,128)(2,1)S(1)}, bf16[256,1024]{0,1:T(8,128)(2,1)}, u32[]{:S(2)}) copy-start(bf16[256,1024]{0,1:T(8,128)(2,1)} %copy.51) | copy-start | bytes 1572868
  24.1 110.4 %all-to-all-start.1 = ((bf16[16,64,1024]{2,1,0:T(8,128)(2,1)}), bf16[16,64,1024]{2,1,0:T(8,128)(2,1)}, u32[]{:S(2)}, u32[]{:S(2)}) async-start(bf16[16,64,1024]{2,1,0:T(8,128)(2,1)} %bitcast.61), calls=%async_computation.1 | async-start | bytes 4194304 | tf_op jit(solution)/shard_map/all_to_all | solution.py:89
  89.7 1.9 %copy-start.2 = (f32[16,256,256]{1,2,0:T(8,128)}, f32[16,256,256]{1,2,0:T(8,128)S(1)}, u32[]{:S(2)}) copy-start(f32[16,256,256]{1,2,0:T(8,128)S(1)} %get-tuple-element.10) | copy-start | bytes 12582916
  89.7 1.9 %copy-start.7 = (bf16[16,1024]{1,0:T(8,128)(2,1)S(1)}, bf16[16,1024]{1,0:T(8,128)(2,1)}, u32[]{:S(2)}) copy-start(bf16[16,1024]{1,0:T(8,128)(2,1)} %param.22) | copy-start | bytes 98308
  89.7 5.4 %copy-start.9 = (s32[16]{0:T(128)S(1)}, s32[16]{0:T(128)}, u32[]{:S(2)}) copy-start(s32[16]{0:T(128)} %param.16) | copy-start | bytes 196
  92.0 9.7 %collective-permute-start.1 = (bf16[32,1024]{0,1:T(8,128)(2,1)S(1)}, bf16[32,1024]{0,1:T(8,128)(2,1)S(1)}, u32[]{:S(2)}, u32[]{:S(2)}) collective-permute-start(bf16[32,1024]{0,1:T(8,128)(2,1)S(1)} %broadcast_select_fusion), channel_id=1, source_target_pairs={{0,2},{1,3},{2,0},{3,1},{4,6},{5,7},{6,4},{7,5},{8,10},{9,11},{10,... | collective-permute-start | bytes 196616 | tf_op jit(solution)/shard_map/ppermute | solution.py:64
  102.1 10.2 %collective-permute-start.2 = (bf16[64,1024]{0,1:T(8,128)(2,1)S(1)}, bf16[64,1024]{0,1:T(8,128)(2,1)S(1)}, u32[]{:S(2)}, u32[]{:S(2)}) collective-permute-start(bf16[64,1024]{0,1:T(8,128)(2,1)S(1)} %maximum_select_fusion.4), channel_id=1, source_target_pairs={{0,4},{1,5},{2,6},{3,7},{4,0},{5,1},{6,2},{7,3},{8,12},{9,13},{10,... | collective-permute-start | bytes 393224 | tf_op jit(solution)/shard_map/ppermute | solution.py:64
  112.6 13.7 %collective-permute-start.3 = (bf16[128,1024]{0,1:T(8,128)(2,1)S(1)}, bf16[128,1024]{0,1:T(8,128)(2,1)S(1)}, u32[]{:S(2)}, u32[]{:S(2)}) collective-permute-start(bf16[128,1024]{0,1:T(8,128)(2,1)S(1)} %maximum_select_fusion.6), channel_id=1, source_target_pairs={{0,8},{1,9},{2,10},{3,11},{4,12},{5,13},{6,14},{7,15},{8,0},{9,1},... | collective-permute-start | bytes 786440 | tf_op jit(solution)/shard_map/ppermute | solution.py:64
  126.3 3.1 %copy-start.3 = (bf16[16,16,1024]{2,1,0:T(8,128)(2,1)S(1)}, bf16[16,16,1024]{2,1,0:T(8,128)(2,1)}, u32[]{:S(2)}) copy-start(bf16[16,16,1024]{2,1,0:T(8,128)(2,1)} %param.14) | copy-start | bytes 1572868
  129.5 1.7 copy-start.11
  130.3 0.8 copy-start.6
  140.3 2.8 %copy-start.10 = (bf16[1024,2048]{1,0:T(8,128)(2,1)S(1)}, bf16[1024,2048]{1,0:T(8,128)(2,1)}, u32[]{:S(2)}) copy-start(bf16[1024,2048]{1,0:T(8,128)(2,1)} %param.25) | copy-start | bytes 12582916
  163.2 6.1 %copy-start.4 = (bf16[16,64,16,64]{3,2,1,0:T(8,128)(2,1)S(1)}, bf16[16,64,16,64]{3,2,1,0:T(8,128)(2,1)}, u32[]{:S(2)}) copy-start(bf16[16,64,16,64]{3,2,1,0:T(8,128)(2,1)} %reshape.198) | copy-start | bytes 6291460
